TPU v7x, 256 devices: a whole 4x4x8 slice. The times are simulated.
256 devices in a mesh: feeder: 32 (over z_hi, y, core), factor: 8 (over z_lo, x).
Axes of the slice: x: 4, y: 4, z: 8 (z_hi: 4, z_lo: 2; z = z_hi * 2 + z_lo), core: 2. Of those that a mesh axis runs over, the one named last changes fastest.
Arguments:
- sensitivity: bfloat16 [32, 2048, 2048], P('feeder'), may hold values from -0.015625 to 0.015625
- headroom: float32 [32, 8, 2048], P('feeder'), may hold values from 0 to 3
- ev_power: float32 [32, 8, 256], P('feeder'), may hold values from 0.5 to 4
- ev_node: int32 [32, 8, 256], P('feeder'), may hold values from 0 to 2047
- region_map: int32 [32, 256], P('feeder'), may hold values from 0 to 511
- loadings: float32 [512, 8, 512], P('feeder', None, 'factor'), may hold values from -8 to 8
Outputs:
- margin: float32 [32, 8, 2048], P('feeder')
- new_loadings: float32 [512, 8, 512], P('feeder', None, 'factor')
All inputs are finite; a program needn't handle non-finite values.
Results may differ from a plain program's by a relative error of at most 0.0031.
Values may be sent and summed in bfloat16 or wider, within the bound.
No kernel may reach another device: no remote copies, remote signals or barrier semaphores. Data moves between devices by JAX's collectives and lax.ppermute only.
A program may use at most 64 MiB of HBM per device.

v0:
```python
import jax
import jax.numpy as jnp
from jax import lax
from jax.sharding import PartitionSpec as P

quantile = 1.645
epsilon = 1e-06
step_size = 16.0


def shards(sensitivity, headroom, ev_power, ev_node, region_map, loadings):
    members = sensitivity.shape[0]
    ev_count = ev_power.shape[2]
    reg_local, hours, columns = loadings.shape
    total_regions = reg_local * lax.axis_size("feeder")
    packed = loadings.astype(jnp.bfloat16).reshape(reg_local, hours * columns)
    regions = region_map.reshape(-1)
    shard_rows = lax.all_gather(packed, "feeder", axis=0, tiled=True)
    row_count = shard_rows.shape[0]
    matches = (regions[:, None] == lax.iota(jnp.int32, row_count)[None, :]).astype(jnp.bfloat16)
    looked = jnp.dot(matches, shard_rows, preferred_element_type=jnp.float32)
    volts_list = []
    rows_list = []
    partial_list = []
    member = 0
    for interval in range(hours):
        block = looked[
            member * ev_count : (member + 1) * ev_count,
            interval * columns : (interval + 1) * columns,
        ]
        weighted = (ev_power[member, interval][:, None] * block).astype(jnp.bfloat16)
        sens_rows = jnp.take(sensitivity[member], ev_node[member, interval], axis=0)
        factor_volts = jnp.dot(weighted.T, sens_rows, preferred_element_type=jnp.float32)
        volts_list.append(factor_volts)
        rows_list.append(sens_rows)
        partial_sum = jnp.sum(factor_volts * factor_volts, axis=0)
        partial_list.append(partial_sum)
    variance = jnp.stack(partial_list, axis=0).reshape(members, hours, -1)
    variance = lax.psum(variance, "factor")
    deviation = jnp.sqrt(variance + epsilon)
    margin = headroom - quantile * deviation
    violation = jnp.maximum(-margin, 0.0)
    var_grad = quantile * violation / deviation
    member = 0
    interval_grads = []
    for interval in range(hours):
        position = member * hours + interval
        volt_grad = (2.0 * var_grad[member, interval][None, :] * volts_list[position]).astype(
            jnp.bfloat16
        )
        weight_grad = jnp.dot(rows_list[position], volt_grad.T, preferred_element_type=jnp.float32)
        interval_grads.append(ev_power[member, interval][:, None] * weight_grad)
    member_grads = jnp.concatenate(interval_grads, axis=1)
    offset = regions - 0
    inside = jnp.logical_and(offset >= 0, offset < total_regions)
    target = jnp.where(inside, offset, total_regions)
    summed = jax.ops.segment_sum(member_grads, target, num_segments=total_regions + 1)
    whole_term = summed[:total_regions]
    reduced = lax.psum_scatter(whole_term, "feeder", scatter_dimension=0, tiled=True)
    new_loadings = loadings - step_size * reduced.reshape(reg_local, hours, columns)
    return (margin, new_loadings)


def solution(mesh):
    return jax.shard_map(
        shards,
        mesh=mesh,
        in_specs=(
            P("feeder", None, None),
            P("feeder", None, None),
            P("feeder", None, None),
            P("feeder", None, None),
            P("feeder", None),
            P("feeder", None, "factor"),
        ),
        out_specs=(P("feeder", None, None), P("feeder", None, "factor")),
        check_vma=False,
    )
```

profile of v0, /device:TPU:2, one launch (start us, length us, event | category | flops | bytes accessed | tf_op | source)
XLA Modules:
  0.0 324.0 jit_solution(15895754559689770932)
XLA Ops:
  7.2 0.0 all-reduce.2.cloned.1.call-start
  7.2 1.0 fusion.61
  8.4 1.0 fusion.60
  9.4 0.8 convert_element_type.52
  10.3 0.1 reshape.133
  10.4 49.2 %all_gather.3 = bf16[512,512]{1,0:T(8,128)(2,1)S(1)} all-gather(bf16[16,512]{1,0:T(8,128)(2,1)S(1)} %reshape.133), channel_id=1, replica_groups=mesh['feeder'=32,'factor'=8] {'feeder'}, dimensions={0}, use_global_device_ids=true | all-gather | bytes 540672 | tf_op jit(solution)/shard_map/all_gather | solution.py:18
  59.6 6.8 %gather_fusion.2 = bf16[256,2048]{1,0:T(8,128)(2,1)S(1)} fusion(bf16[2048,2048]{1,0:T(8,128)(2,1)} %bitcast.39, s32[1024]{0:T(1024)S(1)} %pad_clamp_fusion.5), kind=kCustom, calls=%fused_computation.2.clone | custom fusion | bytes 2098176 | tf_op jit(solution)/shard_map/jit(_take)/gather | solution.py:32
  66.4 6.8 %gather_fusion.3 = bf16[256,2048]{1,0:T(8,128)(2,1)S(1)} fusion(bf16[2048,2048]{1,0:T(8,128)(2,1)} %bitcast.40, s32[1024]{0:T(1024)S(1)} %pad_clamp_fusion.4), kind=kCustom, calls=%fused_computation.3.clone | custom fusion | bytes 2098176 | tf_op jit(solution)/shard_map/jit(_take)/gather | solution.py:32
  73.3 7.8 %gather_fusion.4 = bf16[256,2048]{1,0:T(8,128)(2,1)} fusion(bf16[2048,2048]{1,0:T(8,128)(2,1)} %bitcast.41, s32[1024]{0:T(1024)S(1)} %pad_clamp_fusion.3), kind=kCustom, calls=%fused_computation.4.clone | custom fusion | bytes 2098176 | tf_op jit(solution)/shard_map/jit(_take)/gather | solution.py:32
  81.1 8.0 %gather_fusion.5 = bf16[256,2048]{1,0:T(8,128)(2,1)} fusion(bf16[2048,2048]{1,0:T(8,128)(2,1)} %bitcast.42, s32[1024]{0:T(1024)S(1)} %pad_clamp_fusion.2), kind=kCustom, calls=%fused_computation.5.clone | custom fusion | bytes 2098176 | tf_op jit(solution)/shard_map/jit(_take)/gather | solution.py:32
  89.1 7.8 %gather_fusion.6 = bf16[256,2048]{1,0:T(8,128)(2,1)} fusion(bf16[2048,2048]{1,0:T(8,128)(2,1)} %bitcast.43, s32[1024]{0:T(1024)S(1)} %pad_clamp_fusion.1), kind=kCustom, calls=%fused_computation.6.clone | custom fusion | bytes 2098176 | tf_op jit(solution)/shard_map/jit(_take)/gather | solution.py:32
  96.9 7.8 %gather_fusion.7 = bf16[256,2048]{1,0:T(8,128)(2,1)} fusion(bf16[2048,2048]{1,0:T(8,128)(2,1)} %bitcast.44, s32[1024]{0:T(1024)S(1)} %pad_clamp_fusion), kind=kCustom, calls=%fused_computation.7.clone | custom fusion | bytes 2098176 | tf_op jit(solution)/shard_map/jit(_take)/gather | solution.py:32
  104.7 0.0 copy-start.7
  104.7 7.9 %gather_fusion.1 = bf16[256,2048]{1,0:T(8,128)(2,1)} fusion(bf16[2048,2048]{1,0:T(8,128)(2,1)} %bitcast.45, s32[1024]{0:T(1024)S(1)} %pad_clamp_fusion.6), kind=kCustom, calls=%fused_computation.1.clone | custom fusion | bytes 2098176 | tf_op jit(solution)/shard_map/jit(_take)/gather | solution.py:32
  112.6 8.0 %gather_fusion = bf16[256,2048]{1,0:T(8,128)(2,1)} fusion(bf16[2048,2048]{1,0:T(8,128)(2,1)} %bitcast.46, s32[1024]{0:T(1024)S(1)} %pad_clamp_fusion.7), kind=kCustom, calls=%fused_computation.clone | custom fusion | bytes 2098176 | tf_op jit(solution)/shard_map/jit(_take)/gather | solution.py:32
  120.6 0.0 copy-start.4
  120.6 0.0 copy-start.2
  120.6 0.0 copy-start
  120.6 0.0 copy-start.6
  120.6 0.0 copy-done.7
  120.7 0.3 fusion.2
  121.0 1.2 multiply_reduce_fusion.5
  122.2 1.2 multiply_reduce_fusion.4
  123.5 2.5 multiply_reduce_fusion.3
  126.0 2.6 multiply_reduce_fusion.2
  128.5 2.4 multiply_reduce_fusion.1
  131.0 0.0 copy-done.4
  131.0 1.3 multiply_reduce_fusion
  132.2 0.0 copy-done.2
  132.2 1.3 multiply_reduce_fusion.6
  133.5 0.0 copy-done
  133.5 1.2 multiply_reduce_fusion.7
  134.8 0.7 stack.35
  135.5 0.0 all-reduce.2.cloned.1.call-update
  135.5 0.0 reduce-scatter.2.cloned.1.call-start
  135.6 71.0 %all-reduce.2.cloned.1.call-done = f32[1,8,2048]{2,1,0:T(8,128)} async-done(((f32[1,8,2048]{2,1,0:T(8,128)}), f32[1,8,2048]{2,1,0:T(8,128)}) %all-reduce.2.cloned.1.call-update) | async-done | bytes 65552 | tf_op jit(solution)/shard_map/psum | solution.py:39
  206.5 0.0 copy-done.6
  206.6 1.6 multiply_divide_fusion
  208.2 0.1 slice_multiply_fusion.8
  208.2 0.0 copy-start.1
  208.2 0.0 copy-start.9
  208.3 2.0 convolution_multiply_fusion
  210.2 1.8 convolution_multiply_fusion.1
  212.1 2.5 convolution_multiply_fusion.2
  214.5 2.5 convolution_multiply_fusion.3
  217.1 0.0 copy-done.10
  217.1 1.1 convolution_multiply_fusion.4
  218.2 0.0 copy-done.8
  218.2 0.5 convolution_multiply_fusion.5
  218.7 0.0 copy-done.3
  218.7 0.0 copy-done.11
  218.7 0.5 convolution_multiply_fusion.6
  219.2 0.0 copy-done.1
  219.2 0.0 copy-done.9
  219.3 0.5 convolution_multiply_fusion.7
  219.8 1.3 concatenate.3
  221.1 2.3 scatter_custom_fusion
  223.4 1.1 slice.172
  224.5 0.0 reduce-scatter.2.cloned.1.call-update
  224.5 91.1 %reduce-scatter.2.cloned.1.call-done = f32[16,512]{1,0:T(8,128)} async-done(((f32[512,512]{1,0:T(8,128)}), f32[16,512]{1,0:T(8,128)}) %reduce-scatter.2.cloned.1.call-update) | async-done | bytes 32784 | tf_op jit(solution)/shard_map/reduce_scatter | solution.py:59
  315.6 0.8 broadcast_multiply_fusion
  316.4 0.1 mul.395
  316.5 0.0 copy-done.5
  316.5 0.6 sub.7
  (30 shorter events, 0.2 us)
Async XLA Ops:
  7.2 199.4 %all-reduce.2.cloned.1.call-start = ((), (), s32[]{:S(2)}) async-start(), calls=%async_computation.1 | async-start | bytes 131072 | tf_op jit(solution)/shard_map/psum | solution.py:39
  104.7 15.9 %copy-start.7 = (s32[1,256]{1,0:T(1,128)S(1)}, s32[1,256]{1,0:T(1,128)}, u32[]{:S(2)}) copy-start(s32[1,256]{1,0:T(1,128)} %param.12) | copy-start | bytes 3076
  120.6 10.4 %copy-start.4 = (bf16[256,2048]{1,0:T(8,128)(2,1)S(1)}, bf16[256,2048]{1,0:T(8,128)(2,1)}, u32[]{:S(2)}) copy-start(bf16[256,2048]{1,0:T(8,128)(2,1)} %gather_fusion.7) | copy-start | bytes 3145732
  120.6 11.6 %copy-start.2 = (bf16[256,2048]{1,0:T(8,128)(2,1)S(1)}, bf16[256,2048]{1,0:T(8,128)(2,1)}, u32[]{:S(2)}) copy-start(bf16[256,2048]{1,0:T(8,128)(2,1)} %gather_fusion.1) | copy-start | bytes 3145732
  120.6 12.9 %copy-start = (bf16[256,2048]{1,0:T(8,128)(2,1)S(1)}, bf16[256,2048]{1,0:T(8,128)(2,1)}, u32[]{:S(2)}) copy-start(bf16[256,2048]{1,0:T(8,128)(2,1)} %gather_fusion) | copy-start | bytes 3145732
  120.6 85.9 %copy-start.6 = (f32[1,8,2048]{2,1,0:T(8,128)S(1)}, f32[1,8,2048]{2,1,0:T(8,128)}, u32[]{:S(2)}) copy-start(f32[1,8,2048]{2,1,0:T(8,128)} %param.9) | copy-start | bytes 196612
  133.5 85.2 %copy-start.3 = (bf16[256,2048]{1,0:T(8,128)(2,1)S(1)}, bf16[256,2048]{1,0:T(8,128)(2,1)}, u32[]{:S(2)}) copy-start(bf16[256,2048]{1,0:T(8,128)(2,1)} %gather_fusion.1) | copy-start | bytes 3145732
  135.5 180.1 %reduce-scatter.2.cloned.1.call-start = ((), (), s32[]{:S(2)}) async-start(), calls=%async_computation.2 | async-start | bytes 1081344 | tf_op jit(solution)/shard_map/reduce_scatter | solution.py:59
  206.5 10.5 %copy-start.10 = (f32[64,2048]{1,0:T(8,128)S(1)}, f32[64,2048]{1,0:T(8,128)}, u32[]{:S(2)}) copy-start(f32[64,2048]{1,0:T(8,128)} %get-tuple-element.36) | copy-start | bytes 1572868
  206.5 11.7 %copy-start.8 = (f32[64,2048]{1,0:T(8,128)S(1)}, f32[64,2048]{1,0:T(8,128)}, u32[]{:S(2)}) copy-start(f32[64,2048]{1,0:T(8,128)} %get-tuple-element.34) | copy-start | bytes 1572868
  206.5 12.2 %copy-start.11 = (f32[64,2048]{1,0:T(8,128)S(1)}, f32[64,2048]{1,0:T(8,128)}, u32[]{:S(2)}) copy-start(f32[64,2048]{1,0:T(8,128)} %get-tuple-element.32) | copy-start | bytes 1572868
  208.2 11.0 %copy-start.1 = (bf16[256,2048]{1,0:T(8,128)(2,1)S(1)}, bf16[256,2048]{1,0:T(8,128)(2,1)}, u32[]{:S(2)}) copy-start(bf16[256,2048]{1,0:T(8,128)(2,1)} %gather_fusion) | copy-start | bytes 3145732
  208.2 11.0 %copy-start.9 = (f32[64,2048]{1,0:T(8,128)S(1)}, f32[64,2048]{1,0:T(8,128)}, u32[]{:S(2)}) copy-start(f32[64,2048]{1,0:T(8,128)} %get-tuple-element.30) | copy-start | bytes 1572868
  214.5 101.9 %copy-start.5 = (f32[16,8,64]{2,1,0:T(8,128)S(1)}, f32[16,8,64]{2,1,0:T(8,128)}, u32[]{:S(2)}) copy-start(f32[16,8,64]{2,1,0:T(8,128)} %param.13) | copy-start | bytes 98308
Sparse Core Ops, SparseCore 0:
  135.6 70.8 all-reduce.1
  224.6 90.9 reduce-scatter.1
where the time goes:
time: 325 us; the launch traced here: 324 us
  waiting for transfers between devices  162 us (50%)
  local copies, waits for them, and re-layouts  66.3 us (20%)
  blocking collectives  49.2 us (15%)
  matrix products  25.5 us (8%)
  between operations  14.3 us (4%)
  other arithmetic  6.4 us (2%)
    reduce_scatter x1, waiting for transfers between devices, shards(): lax.psum_scatter(whole_term, 'feeder', scatter_dimension=0, tiled=True)  91.1 us
    psum x1, waiting for transfers between devices, shards(): variance = lax.psum(variance, 'factor')  71 us
    gather x8, local copies, waits for them, and re-layouts, shards(): sens_rows = jnp.take(sensitivity[member], ev_node[member, interval], axis=0)  61 us
    all_gather x1, blocking collectives, shards(): shard_rows = lax.all_gather(packed, 'feeder', axis=0, tiled=True)  49.2 us
    dot_general x8, matrix products, shards(): jnp.dot(weighted.T, sens_rows, preferred_element_type=jnp.float32)  13.7 us
    dot_general x8, matrix products, shards(): jnp.dot(rows_list[position], volt_grad.T, preferred_element_type=jnp.floa...  11.4 us
  transfers between devices with their start and end apart: 2, of which 2 were waited for; matrix products, arithmetic and copies ran while one was open for 0% of the time, Pallas kernels for 0%

commit v1 on v0

--- a/solution.py
+++ b/solution.py
@@ -15,7 +15,10 @@
     total_regions = reg_local * lax.axis_size("feeder")
     packed = loadings.astype(jnp.bfloat16).reshape(reg_local, hours * columns)
     regions = region_map.reshape(-1)
-    shard_rows = lax.all_gather(packed, "feeder", axis=0, tiled=True)
+    r_now = lax.all_to_all(
+        jnp.stack([packed for _ in range(lax.axis_size("feeder"))]), "feeder", 0, 0
+    )
+    shard_rows = jnp.concatenate(r_now, axis=0)
     row_count = shard_rows.shape[0]
     matches = (regions[:, None] == lax.iota(jnp.int32, row_count)[None, :]).astype(jnp.bfloat16)
     looked = jnp.dot(matches, shard_rows, preferred_element_type=jnp.float32)

time: 325 us -> 294 us (0.905)
  blocking collectives: 49.2 us -> 0 us
  starting transfers between devices: 0.08 us -> 11.6 us
  waiting for transfers between devices: 162 us -> 169 us
    all_gather x1 -> x0, blocking collectives: 49.2 us -> none  [shards(): shard_rows = lax.all_gather(packed, 'feeder', axis=0, tiled=True)]
    all_to_all x0 -> x1, starting transfers between devices: none -> 11.5 us  [shards(): lax.all_to_all(jnp.stack([packed for _ in range(lax.axis_size('feeder'))]...]
    psum x1, waiting for transfers between devices: 71 us -> 78.2 us  [shards(): variance = lax.psum(variance, 'factor')]
  transfers between devices with their start and end apart: 2 -> 3, of which waited for: 2 -> 2; matrix products, arithmetic and copies ran while one was open for 0% -> 21% of each run, Pallas kernels for 0% -> 0%
where the time goes in v1:
time: 294 us
  waiting for transfers between devices  169 us (57%)
  local copies, waits for them, and re-layouts  66.2 us (23%)
  matrix products  25.5 us (9%)
  between operations  14.4 us (5%)
  starting transfers between devices  11.6 us (4%)
  other arithmetic  6.41 us (2%)
    reduce_scatter x1, waiting for transfers between devices, shards(): lax.psum_scatter(whole_term, 'feeder', scatter_dimension=0, tiled=True)  91.1 us
    psum x1, waiting for transfers between devices, shards(): variance = lax.psum(variance, 'factor')  78.2 us
    gather x8, local copies, waits for them, and re-layouts, shards(): sens_rows = jnp.take(sensitivity[member], ev_node[member, interval], axis=0)  61 us
    dot_general x8, matrix products, shards(): jnp.dot(weighted.T, sens_rows, preferred_element_type=jnp.float32)  13.7 us
    all_to_all x1, starting transfers between devices, shards(): lax.all_to_all(jnp.stack([packed for _ in range(lax.axis_size('feeder'))]...  11.5 us
    dot_general x8, matrix products, shards(): jnp.dot(rows_list[position], volt_grad.T, preferred_element_type=jnp.floa...  11.4 us
  transfers between devices with their start and end apart: 3, of which 2 were waited for; matrix products, arithmetic and copies ran while one was open for 21% of the time, Pallas kernels for 0%

profile of v1, /device:TPU:2, one launch (start us, length us, event | category | flops | bytes accessed | tf_op | source)
XLA Modules:
  0.0 293.5 jit_solution(11891305600232531640)
XLA Ops:
  7.2 0.8 convert_element_type.52
  8.0 0.1 stack_reshape.2
  8.1 0.9 stack.30
  9.0 11.5 %all-to-all-start = ((bf16[32,16,512]{2,1,0:T(8,128)(2,1)}), bf16[32,16,512]{2,1,0:T(8,128)(2,1)S(1)}, u32[]{:S(2)}, u32[]{:S(2)}) async-start(bf16[32,16,512]{2,1,0:T(8,128)(2,1)} %stack.30), calls=%async_computation | async-start | bytes 1048576 | tf_op jit(solution)/shard_map/all_to_all | solution.py:18
  20.5 0.0 all-reduce.2.cloned.1.call-start
  20.5 1.0 fusion.61
  21.7 6.8 %gather_fusion.2 = bf16[256,2048]{1,0:T(8,128)(2,1)S(1)} fusion(bf16[2048,2048]{1,0:T(8,128)(2,1)} %bitcast.40, s32[1024]{0:T(1024)S(1)} %pad_clamp_fusion.5), kind=kCustom, calls=%fused_computation.2.clone | custom fusion | bytes 2098176 | tf_op jit(solution)/shard_map/jit(_take)/gather | solution.py:35
  28.5 6.8 %gather_fusion.3 = bf16[256,2048]{1,0:T(8,128)(2,1)S(1)} fusion(bf16[2048,2048]{1,0:T(8,128)(2,1)} %bitcast.41, s32[1024]{0:T(1024)S(1)} %pad_clamp_fusion.4), kind=kCustom, calls=%fused_computation.3.clone | custom fusion | bytes 2098176 | tf_op jit(solution)/shard_map/jit(_take)/gather | solution.py:35
  35.3 7.8 %gather_fusion.4 = bf16[256,2048]{1,0:T(8,128)(2,1)} fusion(bf16[2048,2048]{1,0:T(8,128)(2,1)} %bitcast.42, s32[1024]{0:T(1024)S(1)} %pad_clamp_fusion.3), kind=kCustom, calls=%fused_computation.4.clone | custom fusion | bytes 2098176 | tf_op jit(solution)/shard_map/jit(_take)/gather | solution.py:35
  43.2 8.0 %gather_fusion.5 = bf16[256,2048]{1,0:T(8,128)(2,1)} fusion(bf16[2048,2048]{1,0:T(8,128)(2,1)} %bitcast.43, s32[1024]{0:T(1024)S(1)} %pad_clamp_fusion.2), kind=kCustom, calls=%fused_computation.5.clone | custom fusion | bytes 2098176 | tf_op jit(solution)/shard_map/jit(_take)/gather | solution.py:35
  51.2 7.8 %gather_fusion.6 = bf16[256,2048]{1,0:T(8,128)(2,1)} fusion(bf16[2048,2048]{1,0:T(8,128)(2,1)} %bitcast.44, s32[1024]{0:T(1024)S(1)} %pad_clamp_fusion.1), kind=kCustom, calls=%fused_computation.6.clone | custom fusion | bytes 2098176 | tf_op jit(solution)/shard_map/jit(_take)/gather | solution.py:35
  59.0 7.8 %gather_fusion.7 = bf16[256,2048]{1,0:T(8,128)(2,1)} fusion(bf16[2048,2048]{1,0:T(8,128)(2,1)} %bitcast.45, s32[1024]{0:T(1024)S(1)} %pad_clamp_fusion), kind=kCustom, calls=%fused_computation.7.clone | custom fusion | bytes 2098176 | tf_op jit(solution)/shard_map/jit(_take)/gather | solution.py:35
  66.8 0.0 copy-start.7
  66.8 0.0 copy-start.8
  66.8 7.9 %gather_fusion.1 = bf16[256,2048]{1,0:T(8,128)(2,1)} fusion(bf16[2048,2048]{1,0:T(8,128)(2,1)} %bitcast.46, s32[1024]{0:T(1024)S(1)} %pad_clamp_fusion.6), kind=kCustom, calls=%fused_computation.1.clone | custom fusion | bytes 2098176 | tf_op jit(solution)/shard_map/jit(_take)/gather | solution.py:35
  74.7 8.0 %gather_fusion = bf16[256,2048]{1,0:T(8,128)(2,1)} fusion(bf16[2048,2048]{1,0:T(8,128)(2,1)} %bitcast.47, s32[1024]{0:T(1024)S(1)} %pad_clamp_fusion.7), kind=kCustom, calls=%fused_computation.clone | custom fusion | bytes 2098176 | tf_op jit(solution)/shard_map/jit(_take)/gather | solution.py:35
  82.8 0.0 copy-done.7
  82.8 0.0 all-to-all-done
  82.8 0.0 copy-start.4
  82.8 0.0 copy-start.2
  82.9 0.0 copy-start
  82.9 0.0 copy-done.8
  82.9 0.3 fusion.2
  83.2 1.2 multiply_reduce_fusion.5
  84.5 1.2 multiply_reduce_fusion.4
  85.7 2.5 multiply_reduce_fusion.3
  88.2 2.6 multiply_reduce_fusion.2
  90.7 2.5 multiply_reduce_fusion.1
  93.2 0.0 copy-done.4
  93.2 1.2 multiply_reduce_fusion
  94.4 0.0 copy-done.2
  94.4 1.3 multiply_reduce_fusion.6
  95.7 0.0 copy-done
  95.7 1.2 multiply_reduce_fusion.7
  97.0 0.7 stack.39
  97.7 0.0 all-reduce.2.cloned.1.call-update
  97.7 0.0 reduce-scatter.2.cloned.1.call-start
  97.8 78.2 %all-reduce.2.cloned.1.call-done = f32[1,8,2048]{2,1,0:T(8,128)} async-done(((f32[1,8,2048]{2,1,0:T(8,128)}), f32[1,8,2048]{2,1,0:T(8,128)}) %all-reduce.2.cloned.1.call-update) | async-done | bytes 65552 | tf_op jit(solution)/shard_map/psum | solution.py:42
  176.0 0.0 copy-done.6
  176.1 1.6 multiply_divide_fusion
  177.7 0.1 slice_multiply_fusion.8
  177.7 0.0 copy-start.1
  177.7 0.0 copy-start.10
  177.8 2.0 convolution_multiply_fusion
  179.7 1.8 convolution_multiply_fusion.1
  181.6 2.5 convolution_multiply_fusion.2
  184.1 2.5 convolution_multiply_fusion.3
  186.6 0.0 copy-done.11
  186.6 1.2 convolution_multiply_fusion.4
  187.7 0.0 copy-done.9
  187.7 0.5 convolution_multiply_fusion.5
  188.2 0.0 copy-done.3
  188.2 0.0 copy-done.12
  188.3 0.5 convolution_multiply_fusion.6
  188.8 0.0 copy-done.1
  188.8 0.5 convolution_multiply_fusion.7
  189.3 1.3 concatenate.3
  190.6 2.3 scatter_custom_fusion
  193.0 1.1 slice.172
  194.0 0.0 reduce-scatter.2.cloned.1.call-update
  194.0 91.1 %reduce-scatter.2.cloned.1.call-done = f32[16,512]{1,0:T(8,128)} async-done(((f32[512,512]{1,0:T(8,128)}), f32[16,512]{1,0:T(8,128)}) %reduce-scatter.2.cloned.1.call-update) | async-done | bytes 32784 | tf_op jit(solution)/shard_map/reduce_scatter | solution.py:62
  285.2 0.8 broadcast_multiply_fusion
  285.9 0.1 mul.395
  286.0 0.6 sub.7
  (34 shorter events, 0.2 us)
Async XLA Ops:
  9.0 73.8 %all-to-all-start = ((bf16[32,16,512]{2,1,0:T(8,128)(2,1)}), bf16[32,16,512]{2,1,0:T(8,128)(2,1)S(1)}, u32[]{:S(2)}, u32[]{:S(2)}) async-start(bf16[32,16,512]{2,1,0:T(8,128)(2,1)} %stack.30), calls=%async_computation | async-start | bytes 1048576 | tf_op jit(solution)/shard_map/all_to_all | solution.py:18
  20.5 155.6 %all-reduce.2.cloned.1.call-start = ((), (), s32[]{:S(2)}) async-start(), calls=%async_computation.2 | async-start | bytes 131072 | tf_op jit(solution)/shard_map/psum | solution.py:42
  66.8 16.0 %copy-start.7 = (f32[1,8,256]{2,1,0:T(8,128)S(1)}, f32[1,8,256]{2,1,0:T(8,128)}, u32[]{:S(2)}) copy-start(f32[1,8,256]{2,1,0:T(8,128)} %param.10) | copy-start | bytes 24580
  66.8 16.0 %copy-start.8 = (s32[1,256]{1,0:T(1,128)S(1)}, s32[1,256]{1,0:T(1,128)}, u32[]{:S(2)}) copy-start(s32[1,256]{1,0:T(1,128)} %param.12) | copy-start | bytes 3076
  82.7 93.3 %copy-start.6 = (f32[1,8,2048]{2,1,0:T(8,128)S(1)}, f32[1,8,2048]{2,1,0:T(8,128)}, u32[]{:S(2)}) copy-start(f32[1,8,2048]{2,1,0:T(8,128)} %param.9) | copy-start | bytes 196612
  82.8 10.4 %copy-start.4 = (bf16[256,2048]{1,0:T(8,128)(2,1)S(1)}, bf16[256,2048]{1,0:T(8,128)(2,1)}, u32[]{:S(2)}) copy-start(bf16[256,2048]{1,0:T(8,128)(2,1)} %gather_fusion.7) | copy-start | bytes 3145732
  82.8 11.6 %copy-start.2 = (bf16[256,2048]{1,0:T(8,128)(2,1)S(1)}, bf16[256,2048]{1,0:T(8,128)(2,1)}, u32[]{:S(2)}) copy-start(bf16[256,2048]{1,0:T(8,128)(2,1)} %gather_fusion.1) | copy-start | bytes 3145732
  82.9 12.9 %copy-start = (bf16[256,2048]{1,0:T(8,128)(2,1)S(1)}, bf16[256,2048]{1,0:T(8,128)(2,1)}, u32[]{:S(2)}) copy-start(bf16[256,2048]{1,0:T(8,128)(2,1)} %gather_fusion) | copy-start | bytes 3145732
  95.7 92.5 %copy-start.3 = (bf16[256,2048]{1,0:T(8,128)(2,1)S(1)}, bf16[256,2048]{1,0:T(8,128)(2,1)}, u32[]{:S(2)}) copy-start(bf16[256,2048]{1,0:T(8,128)(2,1)} %gather_fusion.1) | copy-start | bytes 3145732
  97.7 187.4 %reduce-scatter.2.cloned.1.call-start = ((), (), s32[]{:S(2)}) async-start(), calls=%async_computation.3 | async-start | bytes 1081344 | tf_op jit(solution)/shard_map/reduce_scatter | solution.py:62
  176.0 10.5 %copy-start.11 = (f32[64,2048]{1,0:T(8,128)S(1)}, f32[64,2048]{1,0:T(8,128)}, u32[]{:S(2)}) copy-start(f32[64,2048]{1,0:T(8,128)} %get-tuple-element.36) | copy-start | bytes 1572868
  176.0 11.7 %copy-start.9 = (f32[64,2048]{1,0:T(8,128)S(1)}, f32[64,2048]{1,0:T(8,128)}, u32[]{:S(2)}) copy-start(f32[64,2048]{1,0:T(8,128)} %get-tuple-element.34) | copy-start | bytes 1572868
  176.0 12.2 %copy-start.12 = (f32[64,2048]{1,0:T(8,128)S(1)}, f32[64,2048]{1,0:T(8,128)}, u32[]{:S(2)}) copy-start(f32[64,2048]{1,0:T(8,128)} %get-tuple-element.32) | copy-start | bytes 1572868
  177.7 11.0 %copy-start.1 = (bf16[256,2048]{1,0:T(8,128)(2,1)S(1)}, bf16[256,2048]{1,0:T(8,128)(2,1)}, u32[]{:S(2)}) copy-start(bf16[256,2048]{1,0:T(8,128)(2,1)} %gather_fusion) | copy-start | bytes 3145732
  177.7 11.0 %copy-start.10 = (f32[64,2048]{1,0:T(8,128)S(1)}, f32[64,2048]{1,0:T(8,128)}, u32[]{:S(2)}) copy-start(f32[64,2048]{1,0:T(8,128)} %get-tuple-element.30) | copy-start | bytes 1572868
  184.1 102.0 %copy-start.5 = (f32[16,8,64]{2,1,0:T(8,128)S(1)}, f32[16,8,64]{2,1,0:T(8,128)}, u32[]{:S(2)}) copy-start(f32[16,8,64]{2,1,0:T(8,128)} %param.13) | copy-start | bytes 98308
Sparse Core Ops, SparseCore 0:
  97.9 78.1 all-reduce.1
  194.2 90.9 reduce-scatter.1
